TPU v7x, 32 devices: a whole 2x2x4 slice. The times are simulated.
32 devices in a mesh: grp: 2 (over y), ctx: 2 (over core), tp: 8 (over z, x).
Axes of the slice: x: 2, y: 2, z: 4, core: 2. Of those that a mesh axis runs over, the one named last changes fastest.
Arguments:
- queries: bfloat16 [8192, 8, 192], P(('grp', 'ctx'), 'tp'), parts along dimension 0, may hold values from -70 to 70
- latent_rows: bfloat16 [8192, 576], P(('grp', 'ctx', 'tp')), parts along dimension 0, may hold values from -6 to 6
- doc_ids: int32 [8192], P(('grp', 'ctx', 'tp')), parts along dimension 0, may hold values from 0 to 7, as said below
- key_weight: bfloat16 [512, 1024], P(None, 'tp'), may hold values from -0.25 to 0.25
- value_weight: bfloat16 [512, 1024], P(None, 'tp'), may hold values from -0.25 to 0.25
Outputs:
- attended: bfloat16 [8192, 1024], P(('grp', 'ctx'), 'tp'), parts along dimension 0
There are 2 independent parts, one for each index of `grp`. A program takes and returns all parts, laid end to end along the dimension named above; an argument that names none is the same for every part. Nothing has to cross between parts.
Inputs may be any that keep to these rules, and one draw needn't show every extreme that they name: `doc_ids`: never falling along the tokens.
All inputs are finite; a program needn't handle non-finite values.
Results may differ from a plain program's by a relative error of at most 0.0065.
Values may be sent and summed in bfloat16 or wider, within the bound.
No kernel may reach another device: no remote copies, remote signals or barrier semaphores. Data moves between devices by JAX's collectives and lax.ppermute only.
A program may use at most 64 MiB of HBM per device.

v0:
```python
import math

import jax
import jax.numpy as jnp
from jax import lax
from jax.sharding import PartitionSpec as P

KV_RANK = 512
ROPE_DIM = 64
NOPE_DIM = 128


def passed_along(block, axis, distance):
    devices = range(lax.axis_size(axis))
    route = [(i - distance, i) for i in devices if i - distance in devices]
    return lax.ppermute(block, axis, route)


def project(gathered, key_weight, value_weight):
    count = gathered.shape[0]
    latent_part = gathered[:, :KV_RANK]
    heads_here = key_weight.shape[1] // NOPE_DIM
    value_width = value_weight.shape[1] // heads_here
    key_heads = jnp.dot(latent_part, key_weight, preferred_element_type=jnp.float32).astype(
        jnp.bfloat16
    )
    value_heads = jnp.dot(latent_part, value_weight, preferred_element_type=jnp.float32).astype(
        jnp.bfloat16
    )
    key_heads = jnp.transpose(key_heads.reshape(count, heads_here, NOPE_DIM), (1, 0, 2))
    value_heads = jnp.transpose(value_heads.reshape(count, heads_here, value_width), (1, 0, 2))
    return (key_heads, value_heads, gathered[:, KV_RANK:])


def attend(queries, query_pos, query_docs, key_sets):
    block_rows = queries.shape[0]
    heads_here = queries.shape[1]
    value_width = key_sets[0][1].shape[2]
    tile_rows = min(512, block_rows)
    tile_count = block_rows // tile_rows
    factor = 1.0 / math.sqrt(NOPE_DIM + ROPE_DIM)
    query_heads = jnp.transpose(queries, (1, 0, 2)).reshape(
        heads_here, tile_count, tile_rows, queries.shape[2]
    )
    pos_tiles = query_pos.reshape(tile_count, tile_rows)
    doc_tiles = query_docs.reshape(tile_count, tile_rows)

    def one_head(packed):
        query_one, key_list, value_list = packed

        def one_tile(tile_pack):
            query_tile, tile_pos, tile_docs = tile_pack
            maxima = jnp.full((tile_rows,), -1e30, jnp.float32)
            totals = jnp.zeros((tile_rows,), jnp.float32)
            summed = jnp.zeros((tile_rows, value_width), jnp.float32)
            for number in range(len(key_sets)):
                key_all = key_list[number]
                value_all = value_list[number]
                rope_all = key_sets[number][2]
                docs_all = key_sets[number][3]
                pos_all = key_sets[number][4]
                length = key_all.shape[0]
                key_rows = min(512, length)
                for begin in range(0, length, key_rows):
                    key_tile = key_all[begin : begin + key_rows]
                    rope_tile = rope_all[begin : begin + key_rows]
                    scores = jnp.dot(
                        query_tile[:, :NOPE_DIM], key_tile.T, preferred_element_type=jnp.float32
                    )
                    scores = scores + jnp.dot(
                        query_tile[:, NOPE_DIM:], rope_tile.T, preferred_element_type=jnp.float32
                    )
                    scores = scores * factor
                    visible = (pos_all[None, begin : begin + key_rows] <= tile_pos[:, None]) & (
                        docs_all[None, begin : begin + key_rows] == tile_docs[:, None]
                    )
                    scores = jnp.where(visible, scores, jnp.float32(-1e30))
                    new_maxima = jnp.maximum(maxima, jnp.max(scores, axis=1))
                    rescale = jnp.exp(maxima - new_maxima)
                    weights = jnp.where(
                        visible, jnp.exp(scores - new_maxima[:, None]), jnp.float32(0.0)
                    )
                    totals = totals * rescale + jnp.sum(weights, axis=1)
                    summed = summed * rescale[:, None] + jnp.dot(
                        weights.astype(jnp.bfloat16),
                        value_all[begin : begin + key_rows],
                        preferred_element_type=jnp.float32,
                    )
                    maxima = new_maxima
            return (summed / totals[:, None]).astype(jnp.bfloat16)

        return lax.map(one_tile, (query_one, pos_tiles, doc_tiles))

    key_lists = tuple((entry[0] for entry in key_sets))
    value_lists = tuple((entry[1] for entry in key_sets))
    result = lax.map(one_head, (query_heads, key_lists, value_lists))
    result = result.reshape(heads_here, block_rows, value_width)
    return jnp.transpose(result, (1, 0, 2)).reshape(block_rows, heads_here * value_width)


def body(queries, latent_rows, doc_ids, key_weight, value_weight):
    block_rows = queries.shape[0]
    cycle_size = lax.axis_size("ctx")
    cycle_index = lax.axis_index("ctx")
    offsets = jnp.arange(block_rows, dtype=jnp.int32)
    query_pos = cycle_index * block_rows + offsets
    gathered, own_docs = (
        lax.all_gather(latent_rows, "tp", axis=0, tiled=True),
        lax.all_gather(doc_ids, "tp", axis=0, tiled=True),
    )
    key_heads, value_heads, rope_keys = project(gathered, key_weight, value_weight)
    key_sets = [(key_heads, value_heads, rope_keys, own_docs, query_pos)]
    moving_keys, moving_values, moving_rope, moving_docs = (
        key_heads,
        value_heads,
        rope_keys,
        own_docs,
    )
    moving_keys, moving_values, moving_rope, moving_docs = passed_along(
        (moving_keys, moving_values, moving_rope, moving_docs), "ctx", 1
    )
    source = (cycle_index - 1) % cycle_size
    key_sets.append(
        (moving_keys, moving_values, moving_rope, moving_docs, source * block_rows + offsets)
    )
    return attend(queries, query_pos, own_docs, key_sets)


def solution(mesh):
    placed = (
        P(("grp", "ctx"), "tp", None),
        P(("grp", "ctx", "tp"), None),
        P(("grp", "ctx", "tp")),
        P(None, "tp"),
        P(None, "tp"),
    )
    return jax.shard_map(
        body, mesh=mesh, in_specs=placed, out_specs=P(("grp", "ctx"), "tp"), check_vma=False
    )
```

profile of v0, /device:TPU:0, one launch (start us, length us, event | category | flops | bytes accessed | tf_op | source)
XLA Modules:
  0.0 189.9 jit_solution(10066499171351850689)
XLA Ops:
  6.5 1.9 %copy.9 = bf16[256,576]{1,0:T(8,128)(2,1)} copy(bf16[256,576]{0,1:T(8,128)(2,1)} %param.8) | data formatting | bytes 589824 | tf_op args[1]
  8.5 58.5 %all-gather.3.cloned.1.call-done = bf16[2048,576]{1,0:T(8,128)(2,1)} async-done(((bf16[256,576]{1,0:T(8,128)(2,1)}), bf16[2048,576]{1,0:T(8,128)(2,1)}) %all-gather.3.cloned.1.call-update) | async-done | bytes 2359312 | tf_op jit(solution)/shard_map/all_gather | solution.py:108
  66.9 3.3 %convolution_convert_fusion = bf16[2048,128]{1,0:T(8,128)(2,1)} fusion(bf16[512,128]{1,0:T(8,128)(2,1)S(1)} %copy-done, bf16[2048,576]{1,0:T(8,128)(2,1)} %all-gather.3.cloned.1.call-done), kind=kOutput, calls=%fused_computation.193 | convolution fusion | flops 268697600 | bytes 2752512 | tf_op jit(solution)/shard_map/dot_general | solution.py:27
  70.2 2.2 %collective-permute-start.3 = (bf16[1,2048,128]{2,1,0:T(8,128)(2,1)}, bf16[1,2048,128]{2,1,0:T(8,128)(2,1)}, u32[]{:S(2)}, u32[]{:S(2)}) collective-permute-start(bf16[1,2048,128]{2,1,0:T(8,128)(2,1)} %bitcast.9), channel_id=1, source_target_pairs={{0,8},{1,9},{2,10},{3,11},{4,12},{5,13},{6,14},{7,15},{16,24},{17,... | collective-permute-start | bytes 1572872 | tf_op jit(solution)/shard_map/ppermute | solution.py:16
  72.4 0.7 convolution_convert_fusion.1
  73.1 1.3 collective-permute-start.1
  74.5 1.3 collective-permute-start.2
  75.8 18.6 %all-gather = s32[8,1,256]{2,1,0:T(1,128)S(1)} all-gather(s32[1,1,256]{2,1,0:T(1,128)S(1)} %bitcast.67), channel_id=1, replica_groups=mesh['grp'=2,'ctx'=2,'tp'=8] {'tp'}, dimensions={0}, use_global_device_ids=true | all-gather | bytes 9216 | tf_op jit(solution)/shard_map/all_gather | solution.py:109
  94.4 1.3 collective-permute-start
  95.8 1.4 copy.8
  97.3 85.8 %while.17 = (s32[]{:T(128)}, bf16[4,512,128]{2,1,0:T(8,128)(2,1)}, s32[2048]{0:T(1024)S(1)}, s32[4,512]{1,0:T(4,128)S(1)}, s32[2048]{0:T(1024)S(1)}, /*index=5*/...) while((s32[]{:T(128)}, bf16[4,512,128]{2,1,0:T(8,128)(2,1)}, ...), condition=%wide.region_17.18_spmd, body=%wide.region_0.17_spmd.sunk | while | flops 1383147008 | bytes 51794588 | solution.py:92
  102.8 0.4 fusion.269
  103.3 1.5 fusion.287
  104.8 1.5 fusion.286
  106.4 1.4 fusion.288
  107.8 1.5 fusion.289
  109.3 1.5 fusion.290
  110.8 1.5 fusion.291
  112.2 1.5 fusion.292
  113.7 1.5 fusion.293
  115.1 1.5 fusion.294
  116.6 2.2 %fusion.295 = bf16[4,512,128]{2,1,0:T(8,128)(2,1)} fusion(bf16[4,512,128]{2,1,0:T(8,128)(2,1)} %get-tuple-element.453, s32[]{:T(128)} %get-tuple-element.452, f32[512,128]{1,0:T(8,128)S(1)} %fusion.294, f32[512,512]{0,1:T(8,128)S(1)} %get-tuple-element.411, f32[512]{0:T(512)S(1)} %get-tuple-element.412, s32[512]{0:T(512)S(1)} %bitcast.45, ...), kind=kOutput, calls=%fused_computation.42.clone.1 | convolution fusion | flops 68878336 | bytes 1585664 | tf_op jit(solution)/shard_map/while/body/eval_jaxpr/while/body/eval_jaxpr/dot_general | solution.py:84
  119.8 0.4 fusion.274
  120.6 0.4 fusion.276
  122.8 0.4 fusion.282
  124.3 0.4 fusion.269
  124.7 1.5 fusion.287
  126.3 1.5 fusion.286
  127.8 1.4 fusion.288
  129.3 1.5 fusion.289
  130.7 1.5 fusion.290
  132.2 1.5 fusion.291
  133.7 1.5 fusion.292
  135.1 1.5 fusion.293
  136.6 1.5 fusion.294
  138.0 2.2 %fusion.295 = bf16[4,512,128]{2,1,0:T(8,128)(2,1)} fusion(bf16[4,512,128]{2,1,0:T(8,128)(2,1)} %get-tuple-element.453, s32[]{:T(128)} %get-tuple-element.452, f32[512,128]{1,0:T(8,128)S(1)} %fusion.294, f32[512,512]{0,1:T(8,128)S(1)} %get-tuple-element.411, f32[512]{0:T(512)S(1)} %get-tuple-element.412, s32[512]{0:T(512)S(1)} %bitcast.45, ...), kind=kOutput, calls=%fused_computation.42.clone.1 | convolution fusion | flops 68878336 | bytes 1585664 | tf_op jit(solution)/shard_map/while/body/eval_jaxpr/while/body/eval_jaxpr/dot_general | solution.py:84
  141.3 0.4 fusion.274
  142.0 0.4 fusion.276
  144.3 0.4 fusion.282
  145.7 0.4 fusion.269
  146.2 1.5 fusion.287
  147.7 1.5 fusion.286
  149.3 1.4 fusion.288
  150.7 1.5 fusion.289
  152.2 1.5 fusion.290
  153.7 1.5 fusion.291
  155.1 1.5 fusion.292
  156.6 1.5 fusion.293
  158.0 1.5 fusion.294
  159.5 2.2 %fusion.295 = bf16[4,512,128]{2,1,0:T(8,128)(2,1)} fusion(bf16[4,512,128]{2,1,0:T(8,128)(2,1)} %get-tuple-element.453, s32[]{:T(128)} %get-tuple-element.452, f32[512,128]{1,0:T(8,128)S(1)} %fusion.294, f32[512,512]{0,1:T(8,128)S(1)} %get-tuple-element.411, f32[512]{0:T(512)S(1)} %get-tuple-element.412, s32[512]{0:T(512)S(1)} %bitcast.45, ...), kind=kOutput, calls=%fused_computation.42.clone.1 | convolution fusion | flops 68878336 | bytes 1585664 | tf_op jit(solution)/shard_map/while/body/eval_jaxpr/while/body/eval_jaxpr/dot_general | solution.py:84
  162.7 0.4 fusion.274
  163.5 0.4 fusion.276
  165.7 0.4 fusion.282
  167.2 0.4 fusion.269
  167.6 1.5 fusion.287
  169.2 1.5 fusion.286
  170.7 1.4 fusion.288
  172.2 1.5 fusion.289
  173.6 1.5 fusion.290
  175.1 1.5 fusion.291
  176.6 1.5 fusion.292
  178.0 1.5 fusion.293
  179.5 1.5 fusion.294
  180.9 2.2 %fusion.295 = bf16[4,512,128]{2,1,0:T(8,128)(2,1)} fusion(bf16[4,512,128]{2,1,0:T(8,128)(2,1)} %get-tuple-element.453, s32[]{:T(128)} %get-tuple-element.452, f32[512,128]{1,0:T(8,128)S(1)} %fusion.294, f32[512,512]{0,1:T(8,128)S(1)} %get-tuple-element.411, f32[512]{0:T(512)S(1)} %get-tuple-element.412, s32[512]{0:T(512)S(1)} %bitcast.45, ...), kind=kOutput, calls=%fused_computation.42.clone.1 | convolution fusion | flops 68878336 | bytes 1585664 | tf_op jit(solution)/shard_map/while/body/eval_jaxpr/while/body/eval_jaxpr/dot_general | solution.py:84
  (95 shorter events, 18.2 us)
Async XLA Ops:
  6.5 60.4 %copy-start = (bf16[512,128]{1,0:T(8,128)(2,1)S(1)}, bf16[512,128]{1,0:T(8,128)(2,1)}, u32[]{:S(2)}) copy-start(bf16[512,128]{1,0:T(8,128)(2,1)} %param.11) | copy-start | bytes 393220
  6.5 65.9 %copy-start.3 = (bf16[512,128]{1,0:T(8,128)(2,1)S(1)}, bf16[512,128]{1,0:T(8,128)(2,1)}, u32[]{:S(2)}) copy-start(bf16[512,128]{1,0:T(8,128)(2,1)} %param.10) | copy-start | bytes 393220
  6.5 60.4 %all-gather.3.cloned.1.call-start = ((), (), s32[]{:S(2)}) async-start(), calls=%async_computation | async-start | bytes 2949120 | tf_op jit(solution)/shard_map/all_gather | solution.py:108
  66.9 5.5 %copy-start.1 = (bf16[2048,576]{1,0:T(8,128)(2,1)S(1)}, bf16[2048,576]{1,0:T(8,128)(2,1)}, u32[]{:S(2)}) copy-start(bf16[2048,576]{1,0:T(8,128)(2,1)} %all-gather.3.cloned.1.call-done) | copy-start | bytes 7077892
  70.2 5.6 %copy-start.2 = (s32[256]{0:T(256)S(1)}, s32[256]{0:T(256)}, u32[]{:S(2)}) copy-start(s32[256]{0:T(256)} %param.9) | copy-start | bytes 3076
  70.2 27.1 %collective-permute-start.3 = (bf16[1,2048,128]{2,1,0:T(8,128)(2,1)}, bf16[1,2048,128]{2,1,0:T(8,128)(2,1)}, u32[]{:S(2)}, u32[]{:S(2)}) collective-permute-start(bf16[1,2048,128]{2,1,0:T(8,128)(2,1)} %bitcast.9), channel_id=1, source_target_pairs={{0,8},{1,9},{2,10},{3,11},{4,12},{5,13},{6,14},{7,15},{16,24},{17,... | collective-permute-start | bytes 1572872 | tf_op jit(solution)/shard_map/ppermute | solution.py:16
  73.1 24.2 %collective-permute-start.1 = (bf16[1,2048,128]{2,1,0:T(8,128)(2,1)S(1)}, bf16[1,2048,128]{2,1,0:T(8,128)(2,1)S(1)}, u32[]{:S(2)}, u32[]{:S(2)}) collective-permute-start(bf16[1,2048,128]{2,1,0:T(8,128)(2,1)S(1)} %bitcast.26), channel_id=1, source_target_pairs={{0,8},{1,9},{2,10},{3,11},{4,12},{5,13},{6,14},{7,15},{16,24},{17,... | collective-permute-start | bytes 1572872 | tf_op jit(solution)/shard_map/ppermute | solution.py:16
  74.5 22.8 %collective-permute-start.2 = (bf16[2048,64]{1,0:T(8,128)(2,1)S(1)}, bf16[2048,64]{1,0:T(8,128)(2,1)S(1)}, u32[]{:S(2)}, u32[]{:S(2)}) collective-permute-start(bf16[2048,64]{1,0:T(8,128)(2,1)S(1)} %slice.151), channel_id=1, source_target_pairs={{0,8},{1,9},{2,10},{3,11},{4,12},{5,13},{6,14},{7,15},{16,24},{17,... | collective-permute-start | bytes 786440 | tf_op jit(solution)/shard_map/ppermute | solution.py:16
  94.4 2.8 %collective-permute-start = (s32[2048]{0:T(1024)S(1)}, s32[2048]{0:T(1024)S(1)}, u32[]{:S(2)}, u32[]{:S(2)}) collective-permute-start(s32[2048]{0:T(1024)S(1)} %bitcast.65), channel_id=1, source_target_pairs={{0,8},{1,9},{2,10},{3,11},{4,12},{5,13},{6,14},{7,15},{16,24},{17,... | collective-permute-start | bytes 24584 | tf_op jit(solution)/shard_map/ppermute | solution.py:16
Sparse Core Ops, SparseCore 0:
  9.5 57.3 all-gather.2
where the time goes:
time: 191 us; the launch traced here: 190 us
  matrix products  76.6 us (40%)
  waiting for transfers between devices  58.5 us (31%)
  blocking collectives  18.6 us (10%)
  between operations  13.5 us (7%)
  other arithmetic  12.4 us (6%)
  starting transfers between devices  6.13 us (3%)
  local copies, waits for them, and re-layouts  3.58 us (2%)
    all_gather x1, waiting for transfers between devices, body(): lax.all_gather(latent_rows, 'tp', axis=0, tiled=True)  58.5 us
    dot_general x32, matrix products, one_tile(): jnp.dot(weights.astype(jnp.bfloat16), value_all[begin:begin + key_rows],...  49.3 us
    all_gather x1, blocking collectives, body(): lax.all_gather(doc_ids, 'tp', axis=0, tiled=True)  18.6 us
    dot_general x32, matrix products, one_tile(): jnp.dot(query_tile[:, NOPE_DIM:], rope_tile.T, preferred_element_type=jnp...  13.9 us
    reduce_sum x8, other arithmetic, one_tile(): totals = totals * rescale + jnp.sum(weights, axis=1)  12.2 us
    dot_general x32, matrix products, one_tile(): jnp.dot(query_tile[:, :NOPE_DIM], key_tile.T, preferred_element_type=jnp....  9.49 us
    ppermute x4, starting transfers between devices, passed_along(): return lax.ppermute(block, axis, route)  6.13 us
  transfers between devices with their start and end apart: 5, of which 1 were waited for; matrix products, arithmetic and copies ran while one was open for 1% of the time, Pallas kernels for 0%

commit v1 on v0

v1 whole, which is shorter than its diff:
```python
import functools
import math

import jax
import jax.numpy as jnp
from jax import lax
from jax.experimental import pallas as pl
from jax.experimental.pallas import tpu as pltpu
from jax.sharding import PartitionSpec as P

KV_RANK = 512
ROPE_DIM = 64
NOPE_DIM = 128
BLOCK_Q = 512
BLOCK_K = 512
FAR = 1 << 30


def passed_along(block, axis, distance):
    devices = range(lax.axis_size(axis))
    route = [(i - distance, i) for i in devices if i - distance in devices]
    return lax.ppermute(block, axis, route)


def flash_kernel(
    lo_ref, hi_ref, qpos_ref, kpos_ref, qdl_ref, kdf_ref,
    q_ref, k_ref, r_ref, v_ref, qd_ref, kd_ref,
    o_ref,
    m_sc, l_sc, acc_sc,
    *, steps, factor,
):
    qt = pl.program_id(1)
    s = pl.program_id(2)
    lo = lo_ref[qt]
    hi = hi_ref[qt]
    kt = jnp.minimum(lo + s, hi)
    bq = q_ref.shape[0]
    bk = k_ref.shape[0]

    @pl.when(s == 0)
    def _():
        m_sc[...] = jnp.full(m_sc.shape, -1e30, jnp.float32)
        l_sc[...] = jnp.zeros(l_sc.shape, jnp.float32)
        acc_sc[...] = jnp.zeros(acc_sc.shape, jnp.float32)

    def tile(masked):
        q = q_ref[...]
        nt = (((1,), (1,)), ((), ()))
        scores = lax.dot_general(
            q[:, :NOPE_DIM], k_ref[...], nt, preferred_element_type=jnp.float32
        )
        scores = scores + lax.dot_general(
            q[:, NOPE_DIM:], r_ref[...], nt, preferred_element_type=jnp.float32
        )
        scores = scores * factor
        if masked:
            qpos = qpos_ref[qt] + lax.broadcasted_iota(jnp.int32, (bq, 1), 0)
            kpos = kpos_ref[kt] + lax.broadcasted_iota(jnp.int32, (1, bk), 1)
            visible = (kpos <= qpos) & (kd_ref[...] == qd_ref[...])
            scores = jnp.where(visible, scores, jnp.float32(-1e30))
        m_prev = m_sc[...]
        m_new = jnp.maximum(m_prev, jnp.max(scores, axis=1, keepdims=True))
        alpha = jnp.exp(m_prev - m_new)
        weights = jnp.exp(scores - m_new)
        if masked:
            weights = jnp.where(visible, weights, jnp.float32(0.0))
        l_sc[...] = alpha * l_sc[...] + jnp.sum(weights, axis=1, keepdims=True)
        acc_sc[...] = alpha * acc_sc[...] + jnp.dot(
            weights.astype(jnp.bfloat16), v_ref[...], preferred_element_type=jnp.float32
        )
        m_sc[...] = m_new

    run = lo + s <= hi
    full = (kpos_ref[kt] + bk - 1 <= qpos_ref[qt]) & (kdf_ref[kt] == qdl_ref[qt])

    @pl.when(run & full)
    def _():
        tile(False)

    @pl.when(run & jnp.logical_not(full))
    def _():
        tile(True)

    @pl.when(s == steps - 1)
    def _():
        o_ref[...] = (acc_sc[...] / l_sc[...]).astype(o_ref.dtype)


def flash(query_heads, keys, ropes, values, query_docs, key_docs, qpos0, kpos0):
    heads_here, rows, _ = query_heads.shape
    count = keys.shape[0]
    value_width = values.shape[1] // heads_here
    bq = min(BLOCK_Q, rows)
    bk = min(BLOCK_K, count)
    q_tiles = rows // bq
    k_tiles = count // bk
    qdf = query_docs[::bq]
    qdl = query_docs[bq - 1 :: bq]
    kdf = key_docs[::bk]
    kdl = key_docs[bk - 1 :: bk]
    active = (kpos0[None, :] <= qpos0[:, None] + (bq - 1)) & (kdl[None, :] >= qdf[:, None])
    index = jnp.arange(k_tiles, dtype=jnp.int32)
    lo = jnp.min(jnp.where(active, index[None, :], k_tiles), axis=1).astype(jnp.int32)
    hi = jnp.max(jnp.where(active, index[None, :], -1), axis=1).astype(jnp.int32)

    def key_map(h, qt, s, lo_ref, hi_ref, *_):
        return (jnp.minimum(lo_ref[qt] + s, hi_ref[qt]), h)

    def rope_map(h, qt, s, lo_ref, hi_ref, *_):
        return (jnp.minimum(lo_ref[qt] + s, hi_ref[qt]), 0)

    def kdoc_map(h, qt, s, lo_ref, hi_ref, *_):
        return (0, jnp.minimum(lo_ref[qt] + s, hi_ref[qt]))

    kernel = functools.partial(
        flash_kernel, steps=k_tiles, factor=1.0 / math.sqrt(NOPE_DIM + ROPE_DIM)
    )
    grid_spec = pltpu.PrefetchScalarGridSpec(
        num_scalar_prefetch=6,
        grid=(heads_here, q_tiles, k_tiles),
        in_specs=[
            pl.BlockSpec((None, bq, query_heads.shape[2]), lambda h, qt, s, *_: (h, qt, 0)),
            pl.BlockSpec((bk, NOPE_DIM), key_map),
            pl.BlockSpec((bk, ROPE_DIM), rope_map),
            pl.BlockSpec((bk, value_width), key_map),
            pl.BlockSpec((bq, 1), lambda h, qt, s, *_: (qt, 0)),
            pl.BlockSpec((1, bk), kdoc_map),
        ],
        out_specs=pl.BlockSpec((bq, value_width), lambda h, qt, s, *_: (qt, h)),
        scratch_shapes=[
            pltpu.VMEM((bq, 1), jnp.float32),
            pltpu.VMEM((bq, 1), jnp.float32),
            pltpu.VMEM((bq, value_width), jnp.float32),
        ],
    )
    return pl.pallas_call(
        kernel,
        grid_spec=grid_spec,
        out_shape=jax.ShapeDtypeStruct((rows, heads_here * value_width), jnp.bfloat16),
        compiler_params=pltpu.CompilerParams(
            dimension_semantics=("arbitrary", "arbitrary", "arbitrary")
        ),
    )(
        lo, hi, qpos0, kpos0, qdl, kdf,
        query_heads, keys, ropes, values,
        query_docs.reshape(rows, 1), key_docs.reshape(1, count),
    )


def body(queries, latent_rows, doc_ids, key_weight, value_weight):
    block_rows = queries.shape[0]
    cycle_size = lax.axis_size("ctx")
    cycle_index = lax.axis_index("ctx")
    gathered, own_docs = (
        lax.all_gather(latent_rows, "tp", axis=0, tiled=True),
        lax.all_gather(doc_ids, "tp", axis=0, tiled=True),
    )
    latent_part = gathered[:, :KV_RANK]
    key_heads = jnp.dot(latent_part, key_weight, preferred_element_type=jnp.float32).astype(
        jnp.bfloat16
    )
    value_heads = jnp.dot(latent_part, value_weight, preferred_element_type=jnp.float32).astype(
        jnp.bfloat16
    )
    rope_keys = gathered[:, KV_RANK:]
    local = (key_heads, value_heads, rope_keys, own_docs)
    sets = []
    for distance in range(cycle_size - 1, 0, -1):
        sets.append(passed_along(local, "ctx", distance))
    sets.append(local)
    keys = jnp.concatenate([entry[0] for entry in sets], axis=0)
    values = jnp.concatenate([entry[1] for entry in sets], axis=0)
    ropes = jnp.concatenate([entry[2] for entry in sets], axis=0)
    key_docs = jnp.concatenate([entry[3] for entry in sets], axis=0)

    bq = min(BLOCK_Q, block_rows)
    bk = min(BLOCK_K, block_rows)
    qpos0 = cycle_index * block_rows + jnp.arange(0, block_rows, bq, dtype=jnp.int32)
    starts = []
    for number in range(cycle_size):
        source = cycle_index - (cycle_size - 1) + number
        tile_starts = source * block_rows + jnp.arange(0, block_rows, bk, dtype=jnp.int32)
        starts.append(jnp.where(source >= 0, tile_starts, FAR))
    kpos0 = jnp.concatenate(starts, axis=0)

    query_heads = jnp.transpose(queries, (1, 0, 2))
    return flash(query_heads, keys, ropes, values, own_docs, key_docs, qpos0, kpos0)


def solution(mesh):
    placed = (
        P(("grp", "ctx"), "tp", None),
        P(("grp", "ctx", "tp"), None),
        P(("grp", "ctx", "tp")),
        P(None, "tp"),
        P(None, "tp"),
    )
    return jax.shard_map(
        body, mesh=mesh, in_specs=placed, out_specs=P(("grp", "ctx"), "tp"), check_vma=False
    )
```

time: 191 us -> 109 us (0.57)
  the two profiles are of different devices: /device:TPU:0 before, /device:TPU:1 now
where the time goes in v1:
time: 109 us; the launch traced here: 107 us
  waiting for transfers between devices  33 us (30%)
  Pallas kernels  23.1 us (21%)
  blocking collectives  18.1 us (17%)
  between operations  13.5 us (12%)
  local copies, waits for them, and re-layouts  6.06 us (6%)
  starting transfers between devices  5.16 us (5%)
  other arithmetic  4.75 us (4%)
  matrix products  3.15 us (3%)
    all_gather x1, waiting for transfers between devices, body(): lax.all_gather(latent_rows, 'tp', axis=0, tiled=True)  30.6 us
    pallas_call x1, Pallas kernels, flash(): pl.pallas_call(kernel, grid_spec=grid_spec, out_shape=jax.ShapeDtypeStruc...  23.1 us
    all_gather x1, blocking collectives, body(): lax.all_gather(doc_ids, 'tp', axis=0, tiled=True)  18.1 us
    ppermute x4, starting transfers between devices, passed_along(): return lax.ppermute(block, axis, route)  5.16 us
    unnamed x14, local copies, waits for them, and re-layouts  3.23 us
    dot_general x1, matrix products, body(): jnp.dot(latent_part, key_weight, preferred_element_type=jnp.float32)  2.44 us
    ppermute x4, waiting for transfers between devices, passed_along(): return lax.ppermute(block, axis, route)  2.33 us
  transfers between devices with their start and end apart: 5, of which 3 were waited for; matrix products, arithmetic and copies ran while one was open for 8% of the time, Pallas kernels for 0%

profile of v1, /device:TPU:1, one launch (start us, length us, event | category | flops | bytes accessed | tf_op | source)
XLA Modules:
  0.0 106.8 jit_solution(16250168030352871523)
XLA Ops:
  6.5 0.0 copy-start
  6.5 0.0 copy-start.1
  6.5 0.0 all-gather.3.cloned.1.call-start
  6.5 1.9 %copy.15 = bf16[256,576]{1,0:T(8,128)(2,1)} copy(bf16[256,576]{0,1:T(8,128)(2,1)} %param.6) | data formatting | bytes 589824 | tf_op args[1]
  8.5 0.0 all-gather.3.cloned.1.call-update
  8.5 18.1 %all-gather = s32[8,1,256]{2,1,0:T(1,128)S(1)} all-gather(s32[1,1,256]{2,1,0:T(1,128)} %bitcast.14), channel_id=1, replica_groups=mesh['grp'=2,'ctx'=2,'tp'=8] {'tp'}, dimensions={0}, use_global_device_ids=true | all-gather | bytes 9216 | tf_op jit(solution)/shard_map/all_gather | solution.py:156
  26.6 1.3 %collective-permute-start = (s32[2048]{0:T(1024)S(1)}, s32[2048]{0:T(1024)S(1)}, u32[]{:S(2)}, u32[]{:S(2)}) collective-permute-start(s32[2048]{0:T(1024)S(1)} %bitcast.8), channel_id=1, source_target_pairs={{0,8},{1,9},{2,10},{3,11},{4,12},{5,13},{6,14},{7,15},{16,24},{17,... | collective-permute-start | bytes 24584 | tf_op jit(solution)/shard_map/ppermute | solution.py:22
  28.0 0.6 broadcast_select_fusion
  28.5 0.1 pad_add_fusion.1.kpos_ref
  28.6 0.0 copy-start.4
  28.6 0.6 slice.20.qdl_ref
  29.2 0.1 slice.19
  29.3 1.4 %copy.16.qd_ref = s32[2048,1]{1,0:T(8,128)} copy(s32[2048,1]{0,1:T(1,128)S(1)} %bitcast.11) | data formatting | bytes 16384 | tf_op jit(solution)/shard_map/reshape | solution.py:146
  30.7 0.0 copy-done.1
  30.7 1.3 %copy.14 = bf16[2048,1,192]{2,0,1:T(8,128)(2,1)} copy(bf16[2048,1,192]{0,2,1:T(8,128)(2,1)S(1)} %copy-done.1) | data formatting | bytes 1572864 | tf_op args[0]
  32.0 1.0 collective-permute-done
  33.0 0.0 copy-start.3
  33.0 0.6 slice.21.kdf_ref
  33.6 0.1 slice.18
  33.7 0.8 select_reduce_fusion
  34.5 0.0 copy-start.5
  34.5 30.6 %all-gather.3.cloned.1.call-done = bf16[2048,576]{1,0:T(8,128)(2,1)} async-done(((bf16[256,576]{1,0:T(8,128)(2,1)}), bf16[2048,576]{1,0:T(8,128)(2,1)}) %all-gather.3.cloned.1.call-update) | async-done | bytes 2359312 | tf_op jit(solution)/shard_map/all_gather | solution.py:155
  65.1 0.0 copy-done
  65.1 0.0 copy-start.2
  65.1 2.4 %convolution_convert_fusion.1 = bf16[2048,128]{1,0:T(8,128)(2,1)S(1)} fusion(bf16[512,128]{1,0:T(8,128)(2,1)S(1)} %copy-done, bf16[2048,576]{1,0:T(8,128)(2,1)} %all-gather.3.cloned.1.call-done), kind=kOutput, calls=%fused_computation.1 | convolution fusion | flops 268697600 | bytes 2752512 | tf_op jit(solution)/shard_map/dot_general | solution.py:159
  67.5 0.0 copy-done.4
  67.5 1.3 %collective-permute-start.1 = (bf16[2048,128]{1,0:T(8,128)(2,1)S(1)}, bf16[2048,128]{1,0:T(8,128)(2,1)S(1)}, u32[]{:S(2)}, u32[]{:S(2)}) collective-permute-start(bf16[2048,128]{1,0:T(8,128)(2,1)S(1)} %convolution_convert_fusion.1), channel_id=1, source_target_pairs={{0,8},{1,9},{2,10},{3,11},{4,12},{5,13},{6,14},{7,15},{16,24},{17,... | collective-permute-start | bytes 1572872 | tf_op jit(solution)/shard_map/ppermute | solution.py:22
  68.8 0.0 copy-done.2
  68.9 0.0 copy-done.3
  68.9 1.3 %collective-permute-start.2 = (bf16[2048,64]{1,0:T(8,128)(2,1)S(1)}, bf16[2048,64]{1,0:T(8,128)(2,1)S(1)}, u32[]{:S(2)}, u32[]{:S(2)}) collective-permute-start(bf16[2048,64]{1,0:T(8,128)(2,1)S(1)} %slice.25), channel_id=1, source_target_pairs={{0,8},{1,9},{2,10},{3,11},{4,12},{5,13},{6,14},{7,15},{16,24},{17,... | collective-permute-start | bytes 786440 | tf_op jit(solution)/shard_map/ppermute | solution.py:22
  70.2 0.0 copy-done.5
  70.2 0.7 convolution_convert_fusion
  70.9 1.3 %collective-permute-start.3 = (bf16[2048,128]{1,0:T(8,128)(2,1)S(1)}, bf16[2048,128]{1,0:T(8,128)(2,1)S(1)}, u32[]{:S(2)}, u32[]{:S(2)}) collective-permute-start(bf16[2048,128]{1,0:T(8,128)(2,1)S(1)} %convolution_convert_fusion), channel_id=1, source_target_pairs={{0,8},{1,9},{2,10},{3,11},{4,12},{5,13},{6,14},{7,15},{16,24},{17,... | collective-permute-start | bytes 1572872 | tf_op jit(solution)/shard_map/ppermute | solution.py:22
  72.2 1.3 %collective-permute-done.2 = bf16[2048,64]{1,0:T(8,128)(2,1)S(1)} collective-permute-done((bf16[2048,64]{1,0:T(8,128)(2,1)S(1)}, bf16[2048,64]{1,0:T(8,128)(2,1)S(1)}, u32[]{:S(2)}, u32[]{:S(2)}) %collective-permute-start.2) | collective-permute-done | bytes 262176 | tf_op jit(solution)/shard_map/ppermute | solution.py:22
  73.6 1.2 %pad_maximum_fusion.1.r_ref = bf16[4096,64]{1,0:T(8,128)(2,1)} fusion(bf16[2048,64]{1,0:T(8,128)(2,1)S(1)} %slice.25, bf16[2048,64]{1,0:T(8,128)(2,1)S(1)} %collective-permute-done.2), kind=kLoop, calls=%fused_computation.5 | loop fusion | flops 1048576 | bytes 1048576 | tf_op jit(solution)/shard_map/concatenate | solution.py:173
  74.8 0.0 collective-permute-done.1
  74.8 1.0 pad_maximum_fusion.k_ref
  75.8 0.0 collective-permute-done.3
  75.8 1.1 pad_maximum_fusion.2.v_ref
  76.9 23.1 %shard_map.55 = bf16[2048,128]{1,0:T(8,128)(2,1)} custom-call(s32[4]{0:T(128)} %get-tuple-element.6.lo_ref, s32[4]{0:T(128)} %get-tuple-element.5.hi_ref, s32[4]{0:T(128)} %get-tuple-element.8.qpos_ref, s32[8]{0:T(128)} %copy-done.4, s32[4]{0:T(128)} %slice.20.qdl_ref, s32[8]{0:T(128)} %slice.21.kdf_ref, bf16[1,2048,192]{2,1,0:T(8,128)(2,1)} %bitcast.7, ...), custom_call_target="tpu_custom_call" | custom-call | tf_op jit(solution)/shard_map/pallas_call | solution.py:136
  (4 shorter events, 0.1 us)
Async XLA Ops:
  6.5 58.5 %copy-start = (bf16[512,128]{1,0:T(8,128)(2,1)S(1)}, bf16[512,128]{1,0:T(8,128)(2,1)}, u32[]{:S(2)}) copy-start(bf16[512,128]{1,0:T(8,128)(2,1)} %param.8) | copy-start | bytes 393220
  6.5 24.2 %copy-start.1 = (bf16[2048,1,192]{0,2,1:T(8,128)(2,1)S(1)}, bf16[2048,1,192]{0,2,1:T(8,128)(2,1)}, u32[]{:S(2)}) copy-start(bf16[2048,1,192]{0,2,1:T(8,128)(2,1)} %param.5) | copy-start | bytes 2359300
  6.5 58.5 %all-gather.3.cloned.1.call-start = ((), (), s32[]{:S(2)}) async-start(), calls=%async_computation | async-start | bytes 2949120 | tf_op jit(solution)/shard_map/all_gather | solution.py:155
  26.6 6.4 %collective-permute-start = (s32[2048]{0:T(1024)S(1)}, s32[2048]{0:T(1024)S(1)}, u32[]{:S(2)}, u32[]{:S(2)}) collective-permute-start(s32[2048]{0:T(1024)S(1)} %bitcast.8), channel_id=1, source_target_pairs={{0,8},{1,9},{2,10},{3,11},{4,12},{5,13},{6,14},{7,15},{16,24},{17,... | collective-permute-start | bytes 24584 | tf_op jit(solution)/shard_map/ppermute | solution.py:22
  28.6 38.9 %copy-start.4 = (s32[8]{0:T(128)}, s32[8]{0:T(128)S(1)}, u32[]{:S(2)}) copy-start(s32[8]{0:T(128)S(1)} %pad_add_fusion.1.kpos_ref) | copy-start | bytes 100
  33.0 35.9 %copy-start.3 = (s32[4096]{0:T(1024)}, s32[4096]{0:T(1024)S(1)}, u32[]{:S(2)}) copy-start(s32[4096]{0:T(1024)S(1)} %pad_add_fusion) | copy-start | bytes 49156
  34.5 35.7 %copy-start.5 = (bf16[512,128]{1,0:T(8,128)(2,1)S(1)}, bf16[512,128]{1,0:T(8,128)(2,1)}, u32[]{:S(2)}) copy-start(bf16[512,128]{1,0:T(8,128)(2,1)} %param.9) | copy-start | bytes 393220
  65.1 3.8 %copy-start.2 = (bf16[2048,576]{1,0:T(8,128)(2,1)S(1)}, bf16[2048,576]{1,0:T(8,128)(2,1)}, u32[]{:S(2)}) copy-start(bf16[2048,576]{1,0:T(8,128)(2,1)} %all-gather.3.cloned.1.call-done) | copy-start | bytes 7077892
  67.5 7.2 %collective-permute-start.1 = (bf16[2048,128]{1,0:T(8,128)(2,1)S(1)}, bf16[2048,128]{1,0:T(8,128)(2,1)S(1)}, u32[]{:S(2)}, u32[]{:S(2)}) collective-permute-start(bf16[2048,128]{1,0:T(8,128)(2,1)S(1)} %convolution_convert_fusion.1), channel_id=1, source_target_pairs={{0,8},{1,9},{2,10},{3,11},{4,12},{5,13},{6,14},{7,15},{16,24},{17,... | collective-permute-start | bytes 1572872 | tf_op jit(solution)/shard_map/ppermute | solution.py:22
  68.9 4.6 %collective-permute-start.2 = (bf16[2048,64]{1,0:T(8,128)(2,1)S(1)}, bf16[2048,64]{1,0:T(8,128)(2,1)S(1)}, u32[]{:S(2)}, u32[]{:S(2)}) collective-permute-start(bf16[2048,64]{1,0:T(8,128)(2,1)S(1)} %slice.25), channel_id=1, source_target_pairs={{0,8},{1,9},{2,10},{3,11},{4,12},{5,13},{6,14},{7,15},{16,24},{17,... | collective-permute-start | bytes 786440 | tf_op jit(solution)/shard_map/ppermute | solution.py:22
  70.9 4.9 %collective-permute-start.3 = (bf16[2048,128]{1,0:T(8,128)(2,1)S(1)}, bf16[2048,128]{1,0:T(8,128)(2,1)S(1)}, u32[]{:S(2)}, u32[]{:S(2)}) collective-permute-start(bf16[2048,128]{1,0:T(8,128)(2,1)S(1)} %convolution_convert_fusion), channel_id=1, source_target_pairs={{0,8},{1,9},{2,10},{3,11},{4,12},{5,13},{6,14},{7,15},{16,24},{17,... | collective-permute-start | bytes 1572872 | tf_op jit(solution)/shard_map/ppermute | solution.py:22
Sparse Core Ops, SparseCore 0:
  9.5 55.4 all-gather.2
